TPU v7x, 256 devices: a whole 4x4x8 slice. The times are simulated.
256 devices in a mesh: req: 64 (over z, x, core), tp: 4 (over y).
Axes of the slice: x: 4, y: 4, z: 8, core: 2. Of those that a mesh axis runs over, the one named last changes fastest.
Arguments:
- hidden: bfloat16 [16384, 2048], P('req'), may hold values from -10.5 to 10.5
- lengths: int32 [64], replicated, may hold values from 1 to 1024, 16384 in all
- dealing: int32 [64], replicated, may hold values from 0 to 63, each once
- norm_gain: bfloat16 [2048], replicated, may hold values from 0.5 to 1.5
- w_query: bfloat16 [2048, 2048], P(None, 'tp'), may hold values from -0.125 to 0.125
- w_key: bfloat16 [2048, 1024], P(None, 'tp'), may hold values from -0.125 to 0.125
- w_value: bfloat16 [2048, 1024], P(None, 'tp'), may hold values from -0.125 to 0.125
- query_gain: bfloat16 [128], replicated, may hold values from 0.5 to 8
- key_gain: bfloat16 [128], replicated, may hold values from 0.5 to 8
- w_out: bfloat16 [2048, 2048], P(None, 'tp'), may hold values from -0.125 to 0.125
Outputs:
- hidden_out: bfloat16 [16384, 2048], P('req', 'tp')
- kv_cache: bfloat16 [2, 64, 1024, 1024], P(None, 'req', None, 'tp')
Inputs may be any that keep to these rules, and one draw needn't show every extreme that they name: The lengths sum to 16384; the largest is exactly 1024. A permutation: dealt slot j, on device j of req, holds prompt dealing[j].
All inputs are finite; a program needn't handle non-finite values.
Results may differ from a plain program's by a relative error of at most 0.012.
The roundings to bfloat16 on the way count: a program that leaves them out, or rounds other values in their place, can miss the bound.
Values may be sent and summed in bfloat16 or wider, within the bound.
No kernel may reach another device: no remote copies, remote signals or barrier semaphores. Data moves between devices by JAX's collectives and lax.ppermute only.
A program may use at most 128 MiB of HBM per device.

v0:
```python
import jax
import jax.numpy as jnp
from jax import lax
from jax.sharding import PartitionSpec as P

EPS = 1e-06
THETA = 1000000.0


def rms_rows(values, scale_gain):
    inv_rms = lax.rsqrt(jnp.mean(values * values, axis=-1, keepdims=True) + EPS)
    return values * inv_rms * scale_gain


def rotate(values, positions):
    features = values.shape[-1]
    half_width = features // 2
    frequency = THETA ** (-(jnp.arange(half_width).astype(jnp.float32) * 2.0) / features)
    angles = positions.astype(jnp.float32)[:, None] * frequency[None, :]
    cosine = jnp.cos(angles)[:, None, :]
    sine_part = jnp.sin(angles)[:, None, :]
    first_half = values[..., :half_width]
    second_half = values[..., half_width:]
    return jnp.concatenate(
        [
            first_half * cosine - second_half * sine_part,
            second_half * cosine + first_half * sine_part,
        ],
        axis=-1,
    )


def project(normed, w_query, w_key, w_value, query_gain, key_gain, positions):
    head_dim = query_gain.shape[0]
    row_count = normed.shape[0]
    query_rows = jnp.dot(normed, w_query, preferred_element_type=jnp.float32).reshape(
        row_count, -1, head_dim
    )
    key_rows = jnp.dot(normed, w_key, preferred_element_type=jnp.float32).reshape(
        row_count, -1, head_dim
    )
    value_rows = jnp.dot(normed, w_value, preferred_element_type=jnp.float32).astype(jnp.bfloat16)
    query_rows = rotate(rms_rows(query_rows, query_gain.astype(jnp.float32)), positions).astype(
        jnp.bfloat16
    )
    key_rows = rotate(rms_rows(key_rows, key_gain.astype(jnp.float32)), positions).astype(
        jnp.bfloat16
    )
    return (query_rows.reshape(row_count, -1), key_rows.reshape(row_count, -1), value_rows)


def attend(query_slot, key_slot, value_slot, prompt_length, head_dim):
    slot_len, query_width = query_slot.shape
    kv_heads = key_slot.shape[1] // head_dim
    group_size = query_width // head_dim // kv_heads
    queries = query_slot.reshape(slot_len, kv_heads, group_size, head_dim)
    keys_split = key_slot.reshape(slot_len, kv_heads, head_dim)
    values_split = value_slot.reshape(slot_len, kv_heads, head_dim)
    scores = jnp.einsum(
        "qkgd,skd->kgqs", queries, keys_split, preferred_element_type=jnp.float32
    ) * head_dim ** (-0.5)
    offsets = jnp.arange(slot_len, dtype=jnp.int32)
    allowed = (offsets[None, :] <= offsets[:, None]) & (offsets[None, :] < prompt_length)
    scores = jnp.where(allowed[None, None], scores, -jnp.inf)
    row_max = jnp.max(scores, axis=-1, keepdims=True)
    weights = jnp.exp(scores - row_max)
    weights = (weights / jnp.sum(weights, axis=-1, keepdims=True)).astype(jnp.bfloat16)
    mixture = jnp.einsum(
        "kgqs,skd->qkgd", weights, values_split, preferred_element_type=jnp.float32
    )
    return mixture.astype(jnp.bfloat16).reshape(slot_len, query_width)


def on_device(
    hidden, lengths, dealing, norm_gain, w_query, w_key, w_value, query_gain, key_gain, w_out
):
    devices = lax.axis_size("req")
    home_index = lax.axis_index("req")
    slice_index = lax.axis_index("tp")
    tok_rows, features = hidden.shape
    head_dim = query_gain.shape[0]
    out_width = w_out.shape[1]
    q_width = w_query.shape[1]
    k_width = w_key.shape[1]
    slot_len = 4 * tok_rows
    capacity = slot_len // devices
    prompt_total = lengths.shape[0]
    prompt_ids = jnp.arange(prompt_total, dtype=jnp.int32)
    prompt_ends = jnp.cumsum(lengths)
    starts = prompt_ends - lengths
    packed_ids = jnp.arange(tok_rows, dtype=jnp.int32) * devices + home_index
    segment = jnp.sum((packed_ids[:, None] >= prompt_ends[None, :]).astype(jnp.int32), axis=1)
    seg_onehot = (segment[:, None] == prompt_ids[None, :]).astype(jnp.int32)
    positions = packed_ids - jnp.sum(seg_onehot * starts[None, :], axis=1)
    inverse = jnp.zeros((prompt_total,), jnp.int32).at[dealing].set(prompt_ids)
    deal_hot = (dealing[:, None] == prompt_ids[None, :]).astype(jnp.int32)
    dealt_starts = jnp.sum(deal_hot * starts[None, :], axis=1)
    dealt_lengths = jnp.sum(deal_hot * lengths[None, :], axis=1)
    first_offset = jnp.mod(home_index - dealt_starts, devices)
    ranks = jnp.arange(capacity, dtype=jnp.int32)
    slot_offset = first_offset[None, :] + ranks[:, None] * devices
    send_valid = slot_offset < dealt_lengths[None, :]
    send_rows = jnp.where(
        send_valid, (dealt_starts[None, :] + slot_offset - home_index) // devices, 0
    ).reshape(-1)
    my_start = lax.dynamic_index_in_dim(dealt_starts, home_index, 0, keepdims=False)
    my_length = lax.dynamic_index_in_dim(dealt_lengths, home_index, 0, keepdims=False)
    roll_shift = jnp.mod(my_start, devices)
    my_slots = jnp.sum(seg_onehot * inverse[None, :], axis=1)
    back_rows = positions // devices * devices + my_slots
    gain_values = norm_gain.astype(jnp.float32)
    normed = rms_rows(hidden.astype(jnp.float32), gain_values).astype(jnp.bfloat16)
    query_rows, key_rows, value_rows = project(
        normed, w_query, w_key, w_value, query_gain, key_gain, positions
    )
    qkv_rows = jnp.concatenate([query_rows, key_rows, value_rows], axis=1)
    picked = jnp.take(qkv_rows, send_rows, axis=0).reshape(capacity, devices, qkv_rows.shape[1])
    arrived = lax.all_to_all(
        jnp.where(send_valid[:, :, None], picked, jnp.zeros((), qkv_rows.dtype)),
        "req",
        split_axis=1,
        concat_axis=1,
        tiled=True,
    )
    slot_rows = jnp.roll(arrived, -roll_shift, axis=1).reshape(slot_len, arrived.shape[2])
    query_slot = slot_rows[:, :q_width]
    key_slot = slot_rows[:, q_width : q_width + k_width]
    value_slot = slot_rows[:, q_width + k_width :]
    mixture = attend(query_slot, key_slot, value_slot, my_length, head_dim)
    sendback = jnp.roll(mixture.reshape(capacity, devices, mixture.shape[1]), roll_shift, axis=1)
    returned = lax.all_to_all(sendback, "req", split_axis=1, concat_axis=1, tiled=True)
    attended = jnp.take(returned.reshape(capacity * devices, -1), back_rows, axis=0)
    kv_cache = jnp.stack([key_slot, value_slot])[:, None]
    summed = jnp.dot(
        lax.all_gather(attended, "tp", axis=1, tiled=True),
        w_out,
        preferred_element_type=jnp.float32,
    )
    branch = lax.optimization_barrier(summed.astype(jnp.bfloat16))
    residual = lax.dynamic_slice_in_dim(hidden, slice_index * out_width, out_width, 1)
    hidden_out = (residual.astype(jnp.float32) + branch.astype(jnp.float32)).astype(jnp.bfloat16)
    return (hidden_out, kv_cache)


def solution(mesh):
    in_specs = (
        P("req", None),
        P(),
        P(),
        P(),
        P(None, "tp"),
        P(None, "tp"),
        P(None, "tp"),
        P(),
        P(),
        P(None, "tp"),
    )
    out_specs = (P("req", "tp"), P(None, "req", None, "tp"))
    return jax.shard_map(
        on_device, mesh=mesh, in_specs=in_specs, out_specs=out_specs, check_vma=False
    )
```

profile of v0, /device:TPU:2, one launch (start us, length us, event | category | flops | bytes accessed | tf_op | source)
XLA Modules:
  0.0 212.4 jit_solution(9252795499204256088)
XLA Ops:
  7.2 0.9 copy.123
  9.0 0.8 select_reduce_fusion.2
  12.7 1.6 fusion.7
  14.3 2.2 %convolution_convert_fusion.1 = bf16[256,256]{0,1:T(8,128)(2,1)S(1)} fusion(bf16[2048,256]{1,0:T(8,128)(2,1)} %param.16, bf16[256,2048]{1,0:T(8,128)(2,1)} %param.10, f32[2048]{0:T(1024)S(1)} %convert_element_type.73, f32[256]{0:T(256)S(1)} %add_rsqrt_fusion.2), kind=kOutput, calls=%fused_computation.30 | convolution fusion | flops 270598144 | bytes 2237440 | tf_op jit(solution)/shard_map/dot_general | solution.py:42
  17.9 2.6 %multiply_reduce_fusion.1 = (f32[256,2]{0,1:T(2,128)S(1)}, f32[256,256]{0,1:T(8,128)}) fusion(bf16[2048,256]{1,0:T(8,128)(2,1)} %param.15, bf16[256,2048]{1,0:T(8,128)(2,1)S(1)} %copy-done.1, f32[2048]{0:T(1024)S(1)} %convert_element_type.73, f32[256]{0:T(256)S(1)} %add_rsqrt_fusion.2), kind=kOutput, calls=%fused_computation.42 | convolution fusion | flops 270663168 | bytes 2370560 | tf_op jit(solution)/shard_map/dot_general | solution.py:39
  23.7 1.1 multiply_multiply_fusion.1
  25.6 2.3 %fusion.29 = f32[256,512]{1,0:T(8,128)} fusion(bf16[2048,512]{1,0:T(8,128)(2,1)S(1)} %copy-done, bf16[256,2048]{1,0:T(8,128)(2,1)S(1)} %copy-done.1, f32[2048]{0:T(1024)} %copy-done.9, f32[256]{0:T(256)} %copy-done.14), kind=kOutput, calls=%fused_computation.107 | convolution fusion | flops 538968064 | bytes 3679232 | tf_op jit(solution)/shard_map/dot_general | solution.py:36
  27.8 1.2 reshape.456
  31.1 5.4 %gather_fusion = bf16[1024,1024]{1,0:T(8,128)(2,1)} fusion(bf16[256,1024]{1,0:T(8,128)(2,1)S(1)} %pad_maximum_fusion, s32[1024]{0:T(1024)S(1)} %broadcast_clamp_fusion), kind=kCustom, calls=%fused_computation | custom fusion | bytes 4198400 | tf_op jit(solution)/shard_map/jit(_take)/gather | solution.py:117
  36.5 4.0 %fusion.11 = bf16[16,64,1024]{2,0,1:T(8,128)(2,1)} fusion(bf16[16,64,1024]{2,1,0:T(8,128)(2,1)} %bitcast.61, pred[16,64]{0,1:T(8,128)(4,1)S(1)} %copy.125, pred[16,64]{0,1:T(8,128)(4,1)S(1)} %copy.124), kind=kLoop, calls=%fused_computation.25 | loop fusion | flops 2097152 | bytes 4196352 | tf_op jit(solution)/shard_map/jit(_where)/select_n | solution.py:119
  40.5 12.4 %all-to-all-start = ((bf16[16,64,1024]{2,0,1:T(8,128)(2,1)}), bf16[16,64,1024]{2,0,1:T(8,128)(2,1)}, u32[]{:S(2)}, u32[]{:S(2)}) async-start(bf16[16,64,1024]{2,0,1:T(8,128)(2,1)} %fusion.11), calls=%async_computation | async-start | bytes 4194304 | tf_op jit(solution)/shard_map/all_to_all | solution.py:118
  56.7 1.3 fusion.6
  58.0 46.0 %all-to-all-done = bf16[16,64,1024]{2,0,1:T(8,128)(2,1)} async-done(((bf16[16,64,1024]{2,0,1:T(8,128)(2,1)}), bf16[16,64,1024]{2,0,1:T(8,128)(2,1)}, u32[]{:S(2)}, u32[]{:S(2)}) %all-to-all-start) | async-done | bytes 2097184 | tf_op jit(solution)/shard_map/all_to_all | solution.py:118
  104.0 2.7 %copy.133 = bf16[16,64,1024]{2,1,0:T(8,128)(2,1)S(1)} copy(bf16[16,64,1024]{2,0,1:T(8,128)(2,1)} %all-to-all-done) | data formatting | bytes 4194304 | tf_op jit(solution)/shard_map/all_to_all | solution.py:118
  106.8 1.6 fusion.10
  108.4 1.4 slice_bitcast_fusion
  109.9 2.0 copy.135
  112.0 2.1 copy.136
  114.0 1.3 copy.137
  115.3 11.2 %fusion.31 = (f32[2,2,1024]{2,1,0:T(2,128)S(1)}, f32[2,2,1024,1024]{2,3,1,0:T(8,128)}) fusion(pred[1024,1024]{0,1:T(8,128)(4,1)} %fusion.6, bf16[1024,2,128,1]{0,2,3,1:T(8,128)(2,1)} %bitcast.68, bf16[1024,2,2,128]{0,3,2,1:T(8,128)(2,1)} %bitcast.65), kind=kOutput, calls=%fused_computation.108 | convolution fusion | flops 1090520064 | bytes 19415040 | tf_op jit(solution)/shard_map/sub | solution.py:66
  126.5 7.2 %fusion.15 = bf16[1024,2,2,128]{0,3,2,1:T(8,128)(2,1)S(1)} fusion(bf16[1024,2,128,1]{0,2,3,1:T(8,128)(2,1)} %bitcast.67, f32[2,2,1024,1024]{2,3,1,0:T(8,128)} %get-tuple-element.35, f32[2,2,1024]{2,1,0:T(2,128)S(1)} %get-tuple-element.34), kind=kOutput, calls=%fused_computation.28 | convolution fusion | flops 1082654720 | bytes 18366464 | tf_op jit(solution)/shard_map/kgqs,skd->qkgd/dot_general | solution.py:68
  133.8 2.0 copy.141
  135.8 1.5 reshape_reshape.3
  138.1 1.5 copy.142
  139.7 5.6 %all-to-all-start.1 = ((bf16[16,64,512]{2,0,1:T(8,128)(2,1)}), bf16[16,64,512]{2,0,1:T(8,128)(2,1)}, u32[]{:S(2)}, u32[]{:S(2)}) async-start(bf16[16,64,512]{2,0,1:T(8,128)(2,1)} %copy.142), calls=%async_computation.1 | async-start | bytes 2097152 | tf_op jit(solution)/shard_map/all_to_all | solution.py:131
  145.4 28.6 %all-to-all-done.1 = bf16[16,64,512]{2,0,1:T(8,128)(2,1)} async-done(((bf16[16,64,512]{2,0,1:T(8,128)(2,1)}), bf16[16,64,512]{2,0,1:T(8,128)(2,1)}, u32[]{:S(2)}, u32[]{:S(2)}) %all-to-all-start.1) | async-done | bytes 1048608 | tf_op jit(solution)/shard_map/all_to_all | solution.py:131
  174.0 1.8 copy.143
  175.8 1.2 gather_fusion.1
  177.8 2.3 %maximum_bitcast_fusion = bf16[2,1,1024,256]{3,2,1,0:T(8,128)(2,1)} fusion(bf16[1,1024,256]{2,1,0:T(8,128)(2,1)} %get-tuple-element.21, bf16[1,1024,256]{2,1,0:T(8,128)(2,1)} %get-tuple-element.20), kind=kLoop, calls=%fused_computation.32 | loop fusion | flops 524288 | bytes 2097152
  180.1 21.2 %all-gather.2.cloned.1.call-done = bf16[256,2048]{1,0:T(8,128)(2,1)} async-done(((bf16[256,512]{1,0:T(8,128)(2,1)}), bf16[256,2048]{1,0:T(8,128)(2,1)}) %all-gather.2.cloned.1.call-update) | async-done | bytes 1048592 | tf_op jit(solution)/shard_map/all_gather | solution.py:135
  201.2 2.6 %convolution_convert_fusion = bf16[256,512]{1,0:T(8,128)(2,1)S(1)} fusion(bf16[256,2048]{1,0:T(8,128)(2,1)} %all-gather.2.cloned.1.call-done, bf16[2048,512]{1,0:T(8,128)(2,1)} %param.19), kind=kOutput, calls=%fused_computation.29 | convolution fusion | flops 537001984 | bytes 3407872 | tf_op jit(solution)/shard_map/dot_general | solution.py:134
  203.8 1.7 add_convert_fusion
  (84 shorter events, 14.7 us)
Async XLA Ops:
  7.2 18.4 %copy-start = (bf16[2048,512]{1,0:T(8,128)(2,1)S(1)}, bf16[2048,512]{1,0:T(8,128)(2,1)}, u32[]{:S(2)}) copy-start(bf16[2048,512]{1,0:T(8,128)(2,1)} %param.14) | copy-start | bytes 6291460
  9.8 2.2 %copy-start.10 = (s32[64]{0:T(128)}, s32[64]{0:T(128)S(1)}, u32[]{:S(2)}) copy-start(s32[64]{0:T(128)S(1)} %get-tuple-element.19) | copy-start | bytes 772
  9.8 7.5 %copy-start.12 = (s32[64]{0:T(128)}, s32[64]{0:T(128)S(1)}, u32[]{:S(2)}) copy-start(s32[64]{0:T(128)S(1)} %get-tuple-element.18) | copy-start | bytes 772
  12.7 5.2 %copy-start.9 = (f32[2048]{0:T(1024)}, f32[2048]{0:T(1024)S(1)}, u32[]{:S(2)}) copy-start(f32[2048]{0:T(1024)S(1)} %convert_element_type.73) | copy-start | bytes 24580
  12.7 4.6 %copy-start.15 = (bf16[128]{0:T(256)(128)(2,1)S(1)}, bf16[128]{0:T(256)(128)(2,1)}, u32[]{:S(2)}) copy-start(bf16[128]{0:T(256)(128)(2,1)} %param.18) | copy-start | bytes 772
  12.7 5.2 %copy-start.1 = (bf16[256,2048]{1,0:T(8,128)(2,1)S(1)}, bf16[256,2048]{1,0:T(8,128)(2,1)}, u32[]{:S(2)}) copy-start(bf16[256,2048]{1,0:T(8,128)(2,1)} %param.10) | copy-start | bytes 3145732
  14.3 6.1 %copy-start.14 = (f32[256]{0:T(256)}, f32[256]{0:T(256)S(1)}, u32[]{:S(2)}) copy-start(f32[256]{0:T(256)S(1)} %add_rsqrt_fusion.2) | copy-start | bytes 3076
  22.6 0.6 copy-start.5
  25.6 3.5 %copy-start.16 = (bf16[128]{0:T(256)(128)(2,1)S(1)}, bf16[128]{0:T(256)(128)(2,1)}, u32[]{:S(2)}) copy-start(bf16[128]{0:T(256)(128)(2,1)} %param.17) | copy-start | bytes 772
  29.4 1.4 copy-start.4
  29.4 1.4 copy-start.8
  29.5 1.5 copy-start.2
  29.5 1.5 copy-start.3
  40.5 12.4 %copy-start.11 = (s32[64]{0:T(128)S(1)}, s32[64]{0:T(128)}, u32[]{:S(2)}) copy-start(s32[64]{0:T(128)} %copy-done.10) | copy-start | bytes 772
  40.5 15.0 %copy-start.13 = (s32[64]{0:T(128)S(1)}, s32[64]{0:T(128)}, u32[]{:S(2)}) copy-start(s32[64]{0:T(128)} %copy-done.12) | copy-start | bytes 772
  40.5 63.5 %all-to-all-start = ((bf16[16,64,1024]{2,0,1:T(8,128)(2,1)}), bf16[16,64,1024]{2,0,1:T(8,128)(2,1)}, u32[]{:S(2)}, u32[]{:S(2)}) async-start(bf16[16,64,1024]{2,0,1:T(8,128)(2,1)} %fusion.11), calls=%async_computation | async-start | bytes 4194304 | tf_op jit(solution)/shard_map/all_to_all | solution.py:118
  138.1 7.3 %copy-start.6 = (s32[256]{0:T(256)S(1)}, s32[256]{0:T(256)}, u32[]{:S(2)}) copy-start(s32[256]{0:T(256)} %copy-done.5) | copy-start | bytes 3076
  138.1 7.3 %copy-start.7 = (s32[256]{0:T(256)S(1)}, s32[256]{0:T(256)}, u32[]{:S(2)}) copy-start(s32[256]{0:T(256)} %get-tuple-element.16) | copy-start | bytes 3076
  139.7 34.3 %all-to-all-start.1 = ((bf16[16,64,512]{2,0,1:T(8,128)(2,1)}), bf16[16,64,512]{2,0,1:T(8,128)(2,1)}, u32[]{:S(2)}, u32[]{:S(2)}) async-start(bf16[16,64,512]{2,0,1:T(8,128)(2,1)} %copy.142), calls=%async_computation.1 | async-start | bytes 2097152 | tf_op jit(solution)/shard_map/all_to_all | solution.py:131
  145.3 55.9 %all-gather.2.cloned.1.call-start = ((), (), s32[]{:S(2)}) async-start(), calls=%async_computation.2 | async-start | bytes 1310720 | tf_op jit(solution)/shard_map/all_gather | solution.py:135
Sparse Core Ops, SparseCore 0:
  177.9 23.2 all-gather.1
where the time goes:
time: 213 us; the launch traced here: 212 us
  waiting for transfers between devices  95.7 us (45%)
  local copies, waits for them, and re-layouts  30.5 us (14%)
  matrix products  28.1 us (13%)
  other arithmetic  23.7 us (11%)
  starting transfers between devices  18 us (8%)
  between operations  16.4 us (8%)
    all_to_all x1, waiting for transfers between devices, on_device(): lax.all_to_all(jnp.where(send_valid[:, :, None], picked, jnp.zeros((), qk...  46 us
    all_to_all x1, waiting for transfers between devices, on_device(): lax.all_to_all(sendback, 'req', split_axis=1, concat_axis=1, tiled=True)  28.6 us
    all_gather x1, waiting for transfers between devices, on_device(): lax.all_gather(attended, 'tp', axis=1, tiled=True)  21.2 us
    all_to_all x1, starting transfers between devices, on_device(): lax.all_to_all(jnp.where(send_valid[:, :, None], picked, jnp.zeros((), qk...  12.4 us
    sub x1, matrix products, attend(): weights = jnp.exp(scores - row_max)  11.2 us
    dot_general x1, matrix products, attend(): jnp.einsum('kgqs,skd->qkgd', weights, values_split, preferred_element_typ...  7.24 us
    all_to_all x1, starting transfers between devices, on_device(): lax.all_to_all(sendback, 'req', split_axis=1, concat_axis=1, tiled=True)  5.63 us
    gather x1, local copies, waits for them, and re-layouts, on_device(): jnp.take(qkv_rows, send_rows, axis=0)  5.39 us
  transfers between devices with their start and end apart: 3, of which 3 were waited for; matrix products, arithmetic and copies ran while one was open for 3% of the time, Pallas kernels for 0%

commit v1 on v0

--- a/solution.py
+++ b/solution.py
@@ -5,6 +5,19 @@
 
 EPS = 1e-06
 THETA = 1000000.0
+
+
+def gather_around(shard, axis, dim):
+    ways = lax.axis_size(axis)
+    up = [(d, (d + 1) % ways) for d in range(ways)]
+    down = [(d, (d - 1) % ways) for d in range(ways)]
+    earlier, later = ([shard], [shard])
+    for _ in range(ways // 2):
+        earlier.append(lax.ppermute(earlier[-1], axis, up))
+    for _ in range((ways - 1) // 2):
+        later.append(lax.ppermute(later[-1], axis, down))
+    line = jnp.concatenate([*earlier[::-1], *later[1:]], axis=dim)
+    return jnp.roll(line, (lax.axis_index(axis) - ways // 2) * shard.shape[dim], axis=dim)
 
 
 def rms_rows(values, scale_gain):
@@ -131,11 +144,7 @@
     returned = lax.all_to_all(sendback, "req", split_axis=1, concat_axis=1, tiled=True)
     attended = jnp.take(returned.reshape(capacity * devices, -1), back_rows, axis=0)
     kv_cache = jnp.stack([key_slot, value_slot])[:, None]
-    summed = jnp.dot(
-        lax.all_gather(attended, "tp", axis=1, tiled=True),
-        w_out,
-        preferred_element_type=jnp.float32,
-    )
+    summed = jnp.dot(gather_around(attended, "tp", 1), w_out, preferred_element_type=jnp.float32)
     branch = lax.optimization_barrier(summed.astype(jnp.bfloat16))
     residual = lax.dynamic_slice_in_dim(hidden, slice_index * out_width, out_width, 1)
     hidden_out = (residual.astype(jnp.float32) + branch.astype(jnp.float32)).astype(jnp.bfloat16)

time: 213 us -> 194 us (0.911); the launches traced: 212 us -> 191 us
  between operations: 16.4 us -> 3.09 us
  waiting for transfers between devices: 95.7 us -> 85 us
  starting transfers between devices: 18 us -> 22.9 us
    all_gather x1 -> x0, waiting for transfers between devices: 21.2 us -> none  [on_device(): lax.all_gather(attended, 'tp', axis=1, tiled=True)]
    ppermute x0 -> x3, waiting for transfers between devices: none -> 10.5 us  [the longest x2 8.85 us: gather_around(): earlier.append(lax.ppermute(earlier[-1], axis, up))]
    ppermute x0 -> x3, starting transfers between devices: none -> 4.89 us  [the longest x1 2.93 us: gather_around(): later.append(lax.ppermute(later[-1], axis, down))]
  transfers between devices with their start and end apart: 3 -> 5, of which waited for: 3 -> 5; matrix products, arithmetic and copies ran while one was open for 3% -> 3% of each run, Pallas kernels for 0% -> 0%
where the time goes in v1:
time: 194 us; the launch traced here: 191 us
  waiting for transfers between devices  85 us (44%)
  local copies, waits for them, and re-layouts  30.6 us (16%)
  matrix products  26.2 us (14%)
  other arithmetic  23.2 us (12%)
  starting transfers between devices  22.9 us (12%)
  between operations  3.09 us (2%)
    all_to_all x1, waiting for transfers between devices, on_device(): lax.all_to_all(jnp.where(send_valid[:, :, None], picked, jnp.zeros((), qk...  46 us
    all_to_all x1, waiting for transfers between devices, on_device(): lax.all_to_all(sendback, 'req', split_axis=1, concat_axis=1, tiled=True)  28.6 us
    all_to_all x1, starting transfers between devices, on_device(): lax.all_to_all(jnp.where(send_valid[:, :, None], picked, jnp.zeros((), qk...  12.4 us
    sub x1, matrix products, attend(): weights = jnp.exp(scores - row_max)  11.2 us
    ppermute x2, waiting for transfers between devices, gather_around(): earlier.append(lax.ppermute(earlier[-1], axis, up))  8.85 us
    dot_general x1, matrix products, attend(): jnp.einsum('kgqs,skd->qkgd', weights, values_split, preferred_element_typ...  7.24 us
    all_to_all x1, starting transfers between devices, on_device(): lax.all_to_all(sendback, 'req', split_axis=1, concat_axis=1, tiled=True)  5.64 us
    gather x1, local copies, waits for them, and re-layouts, on_device(): jnp.take(qkv_rows, send_rows, axis=0)  5.39 us
  transfers between devices with their start and end apart: 5, of which 5 were waited for; matrix products, arithmetic and copies ran while one was open for 3% of the time, Pallas kernels for 0%

profile of v1, /device:TPU:2, one launch (start us, length us, event | category | flops | bytes accessed | tf_op | source)
XLA Modules:
  0.0 191.0 jit_solution(13377544485958813342)
XLA Ops:
  6.2 1.6 fusion.7
  7.8 2.2 %convolution_convert_fusion.1 = bf16[256,256]{0,1:T(8,128)(2,1)S(1)} fusion(bf16[2048,256]{1,0:T(8,128)(2,1)} %param.16, bf16[256,2048]{1,0:T(8,128)(2,1)} %param.10, f32[2048]{0:T(1024)S(1)} %convert_element_type.73, f32[256]{0:T(256)S(1)} %add_rsqrt_fusion.2), kind=kOutput, calls=%fused_computation.30 | convolution fusion | flops 270598144 | bytes 2237440 | tf_op jit(solution)/shard_map/dot_general | solution.py:55
  11.3 2.6 %multiply_reduce_fusion.1 = (f32[256,2]{0,1:T(2,128)S(1)}, f32[256,256]{0,1:T(8,128)}) fusion(bf16[2048,256]{1,0:T(8,128)(2,1)} %param.15, bf16[256,2048]{1,0:T(8,128)(2,1)S(1)} %copy-done.1, f32[2048]{0:T(1024)S(1)} %convert_element_type.73, f32[256]{0:T(256)S(1)} %add_rsqrt_fusion.2), kind=kOutput, calls=%fused_computation.43 | convolution fusion | flops 270663168 | bytes 2370560 | tf_op jit(solution)/shard_map/dot_general | solution.py:52
  19.0 2.3 %fusion.31 = f32[256,512]{1,0:T(8,128)} fusion(bf16[2048,512]{1,0:T(8,128)(2,1)S(1)} %copy-done, bf16[256,2048]{1,0:T(8,128)(2,1)S(1)} %copy-done.1, f32[2048]{0:T(1024)} %copy-done.9, f32[256]{0:T(256)} %copy-done.14), kind=kOutput, calls=%fused_computation.117 | convolution fusion | flops 538968064 | bytes 3679232 | tf_op jit(solution)/shard_map/dot_general | solution.py:49
  21.3 1.2 reshape.456
  24.5 5.4 %gather_fusion = bf16[1024,1024]{1,0:T(8,128)(2,1)} fusion(bf16[256,1024]{1,0:T(8,128)(2,1)S(1)} %pad_maximum_fusion, s32[1024]{0:T(1024)S(1)} %broadcast_clamp_fusion), kind=kCustom, calls=%fused_computation | custom fusion | bytes 4198400 | tf_op jit(solution)/shard_map/jit(_take)/gather | solution.py:130
  29.9 4.0 %fusion.11 = bf16[16,64,1024]{2,0,1:T(8,128)(2,1)} fusion(bf16[16,64,1024]{2,1,0:T(8,128)(2,1)} %bitcast.60, pred[16,64]{0,1:T(8,128)(4,1)S(1)} %copy.125, pred[16,64]{0,1:T(8,128)(4,1)S(1)} %copy.124), kind=kLoop, calls=%fused_computation.25 | loop fusion | flops 2097152 | bytes 4196352 | tf_op jit(solution)/shard_map/jit(_where)/select_n | solution.py:132
  34.0 12.4 %all-to-all-start = ((bf16[16,64,1024]{2,0,1:T(8,128)(2,1)}), bf16[16,64,1024]{2,0,1:T(8,128)(2,1)}, u32[]{:S(2)}, u32[]{:S(2)}) async-start(bf16[16,64,1024]{2,0,1:T(8,128)(2,1)} %fusion.11), calls=%async_computation | async-start | bytes 4194304 | tf_op jit(solution)/shard_map/all_to_all | solution.py:131
  50.2 1.3 fusion.6
  51.5 46.0 %all-to-all-done = bf16[16,64,1024]{2,0,1:T(8,128)(2,1)} async-done(((bf16[16,64,1024]{2,0,1:T(8,128)(2,1)}), bf16[16,64,1024]{2,0,1:T(8,128)(2,1)}, u32[]{:S(2)}, u32[]{:S(2)}) %all-to-all-start) | async-done | bytes 2097184 | tf_op jit(solution)/shard_map/all_to_all | solution.py:131
  97.5 2.7 %copy.133 = bf16[16,64,1024]{2,1,0:T(8,128)(2,1)S(1)} copy(bf16[16,64,1024]{2,0,1:T(8,128)(2,1)} %all-to-all-done) | data formatting | bytes 4194304 | tf_op jit(solution)/shard_map/all_to_all | solution.py:131
  100.2 1.6 fusion.10
  101.8 1.4 slice_bitcast_fusion
  103.4 2.0 %copy.135 = bf16[1024,256]{0,1:T(8,128)(2,1)} copy(bf16[1024,256]{1,0:T(8,128)(2,1)} %get-tuple-element.23) | data formatting | bytes 1048576 | tf_op jit(solution)/shard_map/slice | solution.py:141
  105.4 2.1 %copy.136 = bf16[1024,256]{0,1:T(8,128)(2,1)} copy(bf16[1024,256]{1,0:T(8,128)(2,1)} %get-tuple-element.22) | data formatting | bytes 1048576 | tf_op jit(solution)/shard_map/slice | solution.py:140
  107.5 1.3 copy.137
  108.8 11.2 %fusion.33 = (f32[2,2,1024]{2,1,0:T(2,128)S(1)}, f32[2,2,1024,1024]{2,3,1,0:T(8,128)}) fusion(pred[1024,1024]{0,1:T(8,128)(4,1)} %fusion.6, bf16[1024,2,128,1]{0,2,3,1:T(8,128)(2,1)} %bitcast.67, bf16[1024,2,2,128]{0,3,2,1:T(8,128)(2,1)} %bitcast.64), kind=kOutput, calls=%fused_computation.118 | convolution fusion | flops 1090520064 | bytes 19415040 | tf_op jit(solution)/shard_map/sub | solution.py:79
  120.0 7.2 %fusion.15 = bf16[1024,2,2,128]{0,3,2,1:T(8,128)(2,1)S(1)} fusion(bf16[1024,2,128,1]{0,2,3,1:T(8,128)(2,1)} %bitcast.66, f32[2,2,1024,1024]{2,3,1,0:T(8,128)} %get-tuple-element.35, f32[2,2,1024]{2,1,0:T(2,128)S(1)} %get-tuple-element.34), kind=kOutput, calls=%fused_computation.28 | convolution fusion | flops 1082654720 | bytes 18366464 | tf_op jit(solution)/shard_map/kgqs,skd->qkgd/dot_general | solution.py:81
  127.3 2.0 %copy.141 = bf16[1024,2,2,128]{3,2,1,0:T(2,128)(2,1)} copy(bf16[1024,2,2,128]{0,3,2,1:T(8,128)(2,1)S(1)} %fusion.15) | data formatting | bytes 2097152 | tf_op jit(solution)/shard_map/convert_element_type | solution.py:84
  129.3 1.5 reshape_reshape.3
  131.6 1.5 copy.142
  133.1 5.6 %all-to-all-start.1 = ((bf16[16,64,512]{2,0,1:T(8,128)(2,1)}), bf16[16,64,512]{2,0,1:T(8,128)(2,1)}, u32[]{:S(2)}, u32[]{:S(2)}) async-start(bf16[16,64,512]{2,0,1:T(8,128)(2,1)} %copy.142), calls=%async_computation.1 | async-start | bytes 2097152 | tf_op jit(solution)/shard_map/all_to_all | solution.py:144
  138.9 28.6 %all-to-all-done.1 = bf16[16,64,512]{2,0,1:T(8,128)(2,1)} async-done(((bf16[16,64,512]{2,0,1:T(8,128)(2,1)}), bf16[16,64,512]{2,0,1:T(8,128)(2,1)}, u32[]{:S(2)}, u32[]{:S(2)}) %all-to-all-start.1) | async-done | bytes 1048608 | tf_op jit(solution)/shard_map/all_to_all | solution.py:144
  167.5 1.8 copy.143
  169.3 1.2 gather_fusion.1
  170.5 1.7 collective-permute-start
  172.2 6.8 %collective-permute-done = bf16[256,512]{1,0:T(8,128)(2,1)S(1)} collective-permute-done((bf16[256,512]{1,0:T(8,128)(2,1)S(1)}, bf16[256,512]{1,0:T(8,128)(2,1)S(1)}, u32[]{:S(2)}, u32[]{:S(2)}) %collective-permute-start) | collective-permute-done | bytes 262176 | tf_op jit(solution)/shard_map/ppermute | solution.py:16
  179.3 2.3 %maximum_bitcast_fusion = bf16[2,1,1024,256]{3,2,1,0:T(8,128)(2,1)} fusion(bf16[1,1024,256]{2,1,0:T(8,128)(2,1)} %get-tuple-element.21, bf16[1,1024,256]{2,1,0:T(8,128)(2,1)} %get-tuple-element.20), kind=kLoop, calls=%fused_computation.32 | loop fusion | flops 524288 | bytes 2097152
  181.5 2.9 %collective-permute-start.2 = (bf16[256,512]{1,0:T(8,128)(2,1)S(1)}, bf16[256,512]{1,0:T(8,128)(2,1)S(1)}, u32[]{:S(2)}, u32[]{:S(2)}) collective-permute-start(bf16[256,512]{1,0:T(8,128)(2,1)S(1)} %broadcast_select_fusion), channel_id=1, source_target_pairs={{0,3},{1,0},{2,1},{3,2},{4,7},{5,4},{6,5},{7,6},{8,11},{9,8},{10,9... | collective-permute-start | bytes 786440 | tf_op jit(solution)/shard_map/ppermute | solution.py:18
  184.5 2.1 %collective-permute-done.1 = bf16[256,512]{1,0:T(8,128)(2,1)S(1)} collective-permute-done((bf16[256,512]{1,0:T(8,128)(2,1)S(1)}, bf16[256,512]{1,0:T(8,128)(2,1)S(1)}, u32[]{:S(2)}, u32[]{:S(2)}) %collective-permute-start.1) | collective-permute-done | bytes 262176 | tf_op jit(solution)/shard_map/ppermute | solution.py:16
  186.7 1.6 collective-permute-done.2
  189.3 1.7 add_convert_fusion
  (97 shorter events, 18.1 us)
Async XLA Ops:
  0.6 18.4 %copy-start = (bf16[2048,512]{1,0:T(8,128)(2,1)S(1)}, bf16[2048,512]{1,0:T(8,128)(2,1)}, u32[]{:S(2)}) copy-start(bf16[2048,512]{1,0:T(8,128)(2,1)} %param.14) | copy-start | bytes 6291460
  3.3 2.2 %copy-start.10 = (s32[64]{0:T(128)}, s32[64]{0:T(128)S(1)}, u32[]{:S(2)}) copy-start(s32[64]{0:T(128)S(1)} %get-tuple-element.19) | copy-start | bytes 772
  3.3 7.5 %copy-start.12 = (s32[64]{0:T(128)}, s32[64]{0:T(128)S(1)}, u32[]{:S(2)}) copy-start(s32[64]{0:T(128)S(1)} %get-tuple-element.18) | copy-start | bytes 772
  6.2 5.2 %copy-start.9 = (f32[2048]{0:T(1024)}, f32[2048]{0:T(1024)S(1)}, u32[]{:S(2)}) copy-start(f32[2048]{0:T(1024)S(1)} %convert_element_type.73) | copy-start | bytes 24580
  6.2 4.6 %copy-start.16 = (bf16[128]{0:T(256)(128)(2,1)S(1)}, bf16[128]{0:T(256)(128)(2,1)}, u32[]{:S(2)}) copy-start(bf16[128]{0:T(256)(128)(2,1)} %param.18) | copy-start | bytes 772
  6.2 5.2 %copy-start.1 = (bf16[256,2048]{1,0:T(8,128)(2,1)S(1)}, bf16[256,2048]{1,0:T(8,128)(2,1)}, u32[]{:S(2)}) copy-start(bf16[256,2048]{1,0:T(8,128)(2,1)} %param.10) | copy-start | bytes 3145732
  7.8 6.1 %copy-start.14 = (f32[256]{0:T(256)}, f32[256]{0:T(256)S(1)}, u32[]{:S(2)}) copy-start(f32[256]{0:T(256)S(1)} %add_rsqrt_fusion.2) | copy-start | bytes 3076
  16.0 0.6 copy-start.5
  19.0 3.5 %copy-start.17 = (bf16[128]{0:T(256)(128)(2,1)S(1)}, bf16[128]{0:T(256)(128)(2,1)}, u32[]{:S(2)}) copy-start(bf16[128]{0:T(256)(128)(2,1)} %param.17) | copy-start | bytes 772
  22.9 1.4 copy-start.4
  22.9 1.4 copy-start.8
  22.9 1.5 copy-start.2
  22.9 1.5 copy-start.3
  34.0 12.4 %copy-start.11 = (s32[64]{0:T(128)S(1)}, s32[64]{0:T(128)}, u32[]{:S(2)}) copy-start(s32[64]{0:T(128)} %copy-done.10) | copy-start | bytes 772
  34.0 15.0 %copy-start.13 = (s32[64]{0:T(128)S(1)}, s32[64]{0:T(128)}, u32[]{:S(2)}) copy-start(s32[64]{0:T(128)} %copy-done.12) | copy-start | bytes 772
  34.0 63.5 %all-to-all-start = ((bf16[16,64,1024]{2,0,1:T(8,128)(2,1)}), bf16[16,64,1024]{2,0,1:T(8,128)(2,1)}, u32[]{:S(2)}, u32[]{:S(2)}) async-start(bf16[16,64,1024]{2,0,1:T(8,128)(2,1)} %fusion.11), calls=%async_computation | async-start | bytes 4194304 | tf_op jit(solution)/shard_map/all_to_all | solution.py:131
  131.6 7.2 %copy-start.6 = (s32[256]{0:T(256)S(1)}, s32[256]{0:T(256)}, u32[]{:S(2)}) copy-start(s32[256]{0:T(256)} %copy-done.5) | copy-start | bytes 3076
  131.6 7.2 %copy-start.7 = (s32[256]{0:T(256)S(1)}, s32[256]{0:T(256)}, u32[]{:S(2)}) copy-start(s32[256]{0:T(256)} %get-tuple-element.16) | copy-start | bytes 3076
  133.1 34.3 %all-to-all-start.1 = ((bf16[16,64,512]{2,0,1:T(8,128)(2,1)}), bf16[16,64,512]{2,0,1:T(8,128)(2,1)}, u32[]{:S(2)}, u32[]{:S(2)}) async-start(bf16[16,64,512]{2,0,1:T(8,128)(2,1)} %copy.142), calls=%async_computation.1 | async-start | bytes 2097152 | tf_op jit(solution)/shard_map/all_to_all | solution.py:144
  170.5 8.4 %collective-permute-start = (bf16[256,512]{1,0:T(8,128)(2,1)S(1)}, bf16[256,512]{1,0:T(8,128)(2,1)S(1)}, u32[]{:S(2)}, u32[]{:S(2)}) collective-permute-start(bf16[256,512]{1,0:T(8,128)(2,1)S(1)} %broadcast_select_fusion), channel_id=1, source_target_pairs={{0,1},{1,2},{2,3},{3,0},{4,5},{5,6},{6,7},{7,4},{8,9},{9,10},{10,1... | collective-permute-start | bytes 786440 | tf_op jit(solution)/shard_map/ppermute | solution.py:16
  178.9 7.6 %collective-permute-start.1 = (bf16[256,512]{1,0:T(8,128)(2,1)S(1)}, bf16[256,512]{1,0:T(8,128)(2,1)S(1)}, u32[]{:S(2)}, u32[]{:S(2)}) collective-permute-start(bf16[256,512]{1,0:T(8,128)(2,1)S(1)} %collective-permute-done), channel_id=1, source_target_pairs={{0,1},{1,2},{2,3},{3,0},{4,5},{5,6},{6,7},{7,4},{8,9},{9,10},{10,1... | collective-permute-start | bytes 786440 | tf_op jit(solution)/shard_map/ppermute | solution.py:16
  181.5 7.1 %copy-start.15 = (bf16[2048,512]{1,0:T(8,128)(2,1)S(1)}, bf16[2048,512]{1,0:T(8,128)(2,1)}, u32[]{:S(2)}) copy-start(bf16[2048,512]{1,0:T(8,128)(2,1)} %param.19) | copy-start | bytes 6291460
  181.5 6.8 %collective-permute-start.2 = (bf16[256,512]{1,0:T(8,128)(2,1)S(1)}, bf16[256,512]{1,0:T(8,128)(2,1)S(1)}, u32[]{:S(2)}, u32[]{:S(2)}) collective-permute-start(bf16[256,512]{1,0:T(8,128)(2,1)S(1)} %broadcast_select_fusion), channel_id=1, source_target_pairs={{0,3},{1,0},{2,1},{3,2},{4,7},{5,4},{6,5},{7,6},{8,11},{9,8},{10,9... | collective-permute-start | bytes 786440 | tf_op jit(solution)/shard_map/ppermute | solution.py:18
